TPU v7x, 32 devices: a whole 2x2x4 slice. The times are simulated.
32 devices in a mesh: wave: 4 (over y, core), lev: 4 (over z), cpl: 2 (over x).
Axes of the slice: x: 2, y: 2, z: 4, core: 2. Of those that a mesh axis runs over, the one named last changes fastest.
Arguments:
- spectral: bfloat16 [1280, 2, 4, 24, 1280], P('wave', None, None, 'lev'), may hold values from -0.125 to 0.125
- legendre: bfloat16 [1280, 16, 1280], P('wave', 'cpl'), may hold values from -0.15625 to 0.15625
- wavenumber: int32 [1280], replicated, may hold values from 0 to 1279, each once
- level_weight: float32 [24], P('lev'), may hold values from 0.1 to 1
- source_row: int32 [16], replicated, may hold values from 0 to 14
- row_weight: float32 [16], replicated, may hold values from 0.2 to 0.8
Outputs:
- ocean_flux: float32 [16, 4, 4320], P(('wave', 'cpl'), None, 'lev')
All inputs are finite; a program needn't handle non-finite values.
Results may differ from a plain program's by a relative error of at most 0.0041.
Values may be sent and summed in bfloat16 or wider, within the bound.
No kernel may reach another device: no remote copies, remote signals or barrier semaphores. Data moves between devices by JAX's collectives and lax.ppermute only.
A program may use at most 192 MiB of HBM per device.

v0:
```python
import math
import jax
import jax.numpy as jnp
from jax import lax
from jax.sharding import PartitionSpec as P

NLON = 4320


def phase_angle(phase, lon_total):
    return phase.astype(jnp.float32) * (2.0 * math.pi / lon_total)


def surface_flux(grid_vals, level_weight):
    wind_speed = jnp.sqrt(grid_vals[..., 0, :, :] ** 2 + grid_vals[..., 1, :, :] ** 2 + 0.25)
    return jnp.sum(level_weight[:, None] * wind_speed[..., None, :, :] * grid_vals, axis=-2)


def latitude_order(gathered, wave_count, cpl_count, lat_dev):
    trailing = gathered.shape[1:]
    gathered = gathered.reshape((wave_count, cpl_count, lat_dev) + trailing)
    gathered = jnp.swapaxes(gathered, 0, 1)
    return gathered.reshape((wave_count * cpl_count * lat_dev,) + trailing)


def interpolate(gathered, source, weight_hi):
    lower = jnp.take(gathered, source, axis=0)
    upper = jnp.take(gathered, source + 1, axis=0)
    return (1.0 - weight_hi[:, None, None]) * lower + weight_hi[:, None, None] * upper


def local(spectral, legendre, wavenumber, level_weight, source_row, row_weight):
    slot_count = spectral.shape[0]
    fields = spectral.shape[2]
    levels = spectral.shape[3]
    degree = spectral.shape[4]
    channels = 2 * fields * levels
    wave_count = lax.axis_size("wave")
    cpl_count = lax.axis_size("cpl")
    wave_at = lax.axis_index("wave")
    cpl_at = lax.axis_index("cpl")
    owned_waves = lax.dynamic_slice_in_dim(wavenumber, wave_at * slot_count, slot_count)
    coefficient = spectral.reshape(slot_count, channels, degree)
    in_triangle = (
        lax.broadcasted_iota(jnp.int32, (slot_count, 1, degree), 2)
        < (degree - owned_waves)[:, None, None]
    )
    coefficient = jnp.where(in_triangle, coefficient, jnp.zeros_like(coefficient))
    spec_grid = jnp.einsum(
        "skj,slj->slk", coefficient, legendre, preferred_element_type=jnp.float32
    ).astype(jnp.bfloat16)
    by_latitude = lax.all_to_all(spec_grid, "wave", split_axis=1, concat_axis=0, tiled=True)
    total_slots = by_latitude.shape[0]
    lat_dev = by_latitude.shape[1]
    rows_in = (
        by_latitude.reshape(total_slots, lat_dev, 2, fields * levels)
        .transpose(1, 3, 0, 2)
        .reshape(lat_dev * fields * levels, 2 * total_slots)
    )
    lon_block = NLON // 8
    factor = jnp.where(wavenumber == 0, 1.0, 2.0).astype(jnp.float32)[:, None]
    offsets = jnp.arange(lon_block, dtype=jnp.int32)
    base_angle = phase_angle(wavenumber[:, None] * offsets[None, :] % NLON, NLON)
    base_cos = jnp.cos(base_angle)
    base_sin = jnp.sin(base_angle)

    def one_block(first_lon):
        start_angle = phase_angle(wavenumber * first_lon % NLON, NLON)[:, None]
        start_cos = jnp.cos(start_angle)
        start_sin = jnp.sin(start_angle)
        cos_vals = start_cos * base_cos - start_sin * base_sin
        sin_vals = start_sin * base_cos + start_cos * base_sin
        fourier = (
            jnp.stack([factor * cos_vals, -factor * sin_vals], axis=1)
            .astype(jnp.bfloat16)
            .reshape(2 * total_slots, lon_block)
        )
        grid_vals = jnp.dot(rows_in, fourier, preferred_element_type=jnp.float32).reshape(
            lat_dev, fields, levels, lon_block
        )
        return surface_flux(grid_vals, level_weight)

    block_starts = jnp.arange(8, dtype=jnp.int32) * lon_block
    per_block = lax.map(one_block, block_starts)
    partial_value = per_block.transpose(1, 2, 0, 3).reshape(lat_dev, fields, NLON)
    own_first = (wave_at * cpl_count + cpl_at) * lat_dev
    source = lax.dynamic_slice_in_dim(source_row, own_first, lat_dev)
    weight_hi = lax.dynamic_slice_in_dim(row_weight, own_first, lat_dev)
    strip_width = NLON // lax.axis_size("lev")
    summed = lax.psum(partial_value, "lev")
    gathered = lax.all_gather(summed, ("wave", "cpl"), axis=0, tiled=True)
    gathered = latitude_order(gathered, wave_count, cpl_count, lat_dev)
    gathered = lax.dynamic_slice_in_dim(
        gathered, lax.axis_index("lev") * strip_width, strip_width, 2
    )
    return interpolate(gathered, source, weight_hi)


def solution(mesh):
    placed = (P("wave", None, None, "lev", None), P("wave", "cpl", None), P(), P("lev"), P(), P())
    return jax.shard_map(
        local,
        mesh=mesh,
        in_specs=placed,
        out_specs=P(("wave", "cpl"), None, "lev"),
        check_vma=False,
    )
```

profile of v0, /device:TPU:0, one launch (start us, length us, event | category | flops | bytes accessed | tf_op | source)
XLA Modules:
  0.0 437.1 jit_solution(12876540771261802303)
XLA Ops:
  6.5 0.8 dynamic-slice_subtract_fusion
  7.6 26.6 %copy.16 = bf16[320,2,4,6,1280]{4,0,3,2,1:T(8,128)(2,1)} copy(bf16[320,2,4,6,1280]{4,2,3,1,0:T(4,128)(2,1)} %param.10) | data formatting | bytes 78643200 | tf_op args[0]
  34.2 26.6 %bitcast_select_fusion = bf16[320,48,1280]{2,0,1:T(8,128)(2,1)} fusion(bf16[320,2,4,6,1280]{4,0,3,2,1:T(8,128)(2,1)} %copy.16, pred[320,1280]{1,0:T(8,128)(4,1)S(1)} %iota_compare_fusion), kind=kLoop, calls=%fused_computation.40 | loop fusion | flops 19660800 | bytes 79052800 | tf_op jit(solution)/shard_map/jit(_where)/select_n | solution.py:48
  60.8 47.0 %fusion.31 = bf16[320,8,48]{2,1,0:T(8,128)(2,1)S(1)} fusion(bf16[320,8,1280]{2,1,0:T(8,128)(2,1)} %param.11, bf16[320,48,1280]{2,0,1:T(8,128)(2,1)} %bitcast_select_fusion), kind=kOutput, calls=%fused_computation.45 | convolution fusion | flops 314695680 | bytes 46120960 | tf_op jit(solution)/shard_map/skj,slj->slk/dot_general | solution.py:49
  107.8 1.1 copy.18
  109.0 4.2 all-to-all-start
  113.3 6.3 %all-to-all-done = bf16[320,8,48]{0,2,1:T(8,128)(2,1)S(1)} async-done(((bf16[320,8,48]{0,2,1:T(8,128)(2,1)}), bf16[320,8,48]{0,2,1:T(8,128)(2,1)S(1)}, u32[]{:S(2)}, u32[]{:S(2)}) %all-to-all-start) | async-done | bytes 245792 | tf_op jit(solution)/shard_map/all_to_all | solution.py:52
  120.0 1.7 copy.20
  122.4 0.9 copy.21
  123.3 240.5 %while.14 = (s32[]{:T(128)}, f32[8,2,4,540]{3,2,1,0:T(4,128)}, f32[6]{0:T(128)S(1)}, f32[1280,1]{0,1:T(1,128)S(1)}, s32[8]{0:T(128)S(1)}, /*index=5*/s32[1280]{0...) while((s32[]{:T(128)}, f32[8,2,4,540]{3,2,1,0:T(4,128)}, ...), condition=%wide.region_2.3_spmd.clone.clone, body=%wide.region_0.2_spmd.clone.clone.sunk | while | flops 147317040 | bytes 22999700 | solution.py:84
  124.5 12.4 %fusion.47 = (bf16[1280,1,540]{0,2,1:T(8,128)(2,1)S(1)}, bf16[1280,1,540]{0,2,1:T(8,128)(2,1)S(1)}) fusion(s32[1280]{0:T(1024)S(1)} %get-tuple-element.302, f32[1280]{0:T(1024)S(1)} %get-tuple-element.273, f32[1280]{0:T(1024)S(1)} %get-tuple-element.274, f32[1280]{0:T(1024)S(1)} %reduce.4, f32[1280]{0:T(1024)S(1)} %reduce.5), kind=kLoop, calls=%fused_computation.12.clone.1 | loop fusion | flops 13132800 | bytes 2790400 | tf_op jit(solution)/shard_map/convert
  137.2 7.2 %copy.33 = bf16[1280,2,540]{2,1,0:T(2,128)(2,1)} copy(bf16[1280,2,540]{0,2,1:T(8,128)(2,1)S(1)} %pad_maximum_fusion.2) | data formatting | bytes 5529600 | tf_op jit(solution)/shard_map/while/body/eval_jaxpr/stack | solution.py:74
  144.4 6.6 %convert_element_type.80 = bf16[2560,540]{1,0:T(8,128)(2,1)S(1)} reshape(bf16[1280,2,540]{2,1,0:T(2,128)(2,1)} %copy.33) | data formatting | bytes 5529600 | tf_op jit(solution)/shard_map/while/body/eval_jaxpr/convert_element_type | solution.py:75
  151.0 1.5 convolution_bitcast_fusion.2
  154.6 12.4 %fusion.47 = (bf16[1280,1,540]{0,2,1:T(8,128)(2,1)S(1)}, bf16[1280,1,540]{0,2,1:T(8,128)(2,1)S(1)}) fusion(s32[1280]{0:T(1024)S(1)} %get-tuple-element.302, f32[1280]{0:T(1024)S(1)} %get-tuple-element.273, f32[1280]{0:T(1024)S(1)} %get-tuple-element.274, f32[1280]{0:T(1024)S(1)} %reduce.4, f32[1280]{0:T(1024)S(1)} %reduce.5), kind=kLoop, calls=%fused_computation.12.clone.1 | loop fusion | flops 13132800 | bytes 2790400 | tf_op jit(solution)/shard_map/convert
  167.3 7.2 %copy.33 = bf16[1280,2,540]{2,1,0:T(2,128)(2,1)} copy(bf16[1280,2,540]{0,2,1:T(8,128)(2,1)S(1)} %pad_maximum_fusion.2) | data formatting | bytes 5529600 | tf_op jit(solution)/shard_map/while/body/eval_jaxpr/stack | solution.py:74
  174.5 6.6 %convert_element_type.80 = bf16[2560,540]{1,0:T(8,128)(2,1)S(1)} reshape(bf16[1280,2,540]{2,1,0:T(2,128)(2,1)} %copy.33) | data formatting | bytes 5529600 | tf_op jit(solution)/shard_map/while/body/eval_jaxpr/convert_element_type | solution.py:75
  181.1 1.5 convolution_bitcast_fusion.2
  184.7 12.4 %fusion.47 = (bf16[1280,1,540]{0,2,1:T(8,128)(2,1)S(1)}, bf16[1280,1,540]{0,2,1:T(8,128)(2,1)S(1)}) fusion(s32[1280]{0:T(1024)S(1)} %get-tuple-element.302, f32[1280]{0:T(1024)S(1)} %get-tuple-element.273, f32[1280]{0:T(1024)S(1)} %get-tuple-element.274, f32[1280]{0:T(1024)S(1)} %reduce.4, f32[1280]{0:T(1024)S(1)} %reduce.5), kind=kLoop, calls=%fused_computation.12.clone.1 | loop fusion | flops 13132800 | bytes 2790400 | tf_op jit(solution)/shard_map/convert
  197.3 7.2 %copy.33 = bf16[1280,2,540]{2,1,0:T(2,128)(2,1)} copy(bf16[1280,2,540]{0,2,1:T(8,128)(2,1)S(1)} %pad_maximum_fusion.2) | data formatting | bytes 5529600 | tf_op jit(solution)/shard_map/while/body/eval_jaxpr/stack | solution.py:74
  204.5 6.6 %convert_element_type.80 = bf16[2560,540]{1,0:T(8,128)(2,1)S(1)} reshape(bf16[1280,2,540]{2,1,0:T(2,128)(2,1)} %copy.33) | data formatting | bytes 5529600 | tf_op jit(solution)/shard_map/while/body/eval_jaxpr/convert_element_type | solution.py:75
  211.2 1.5 convolution_bitcast_fusion.2
  214.7 12.4 %fusion.47 = (bf16[1280,1,540]{0,2,1:T(8,128)(2,1)S(1)}, bf16[1280,1,540]{0,2,1:T(8,128)(2,1)S(1)}) fusion(s32[1280]{0:T(1024)S(1)} %get-tuple-element.302, f32[1280]{0:T(1024)S(1)} %get-tuple-element.273, f32[1280]{0:T(1024)S(1)} %get-tuple-element.274, f32[1280]{0:T(1024)S(1)} %reduce.4, f32[1280]{0:T(1024)S(1)} %reduce.5), kind=kLoop, calls=%fused_computation.12.clone.1 | loop fusion | flops 13132800 | bytes 2790400 | tf_op jit(solution)/shard_map/convert
  227.4 7.2 %copy.33 = bf16[1280,2,540]{2,1,0:T(2,128)(2,1)} copy(bf16[1280,2,540]{0,2,1:T(8,128)(2,1)S(1)} %pad_maximum_fusion.2) | data formatting | bytes 5529600 | tf_op jit(solution)/shard_map/while/body/eval_jaxpr/stack | solution.py:74
  234.6 6.6 %convert_element_type.80 = bf16[2560,540]{1,0:T(8,128)(2,1)S(1)} reshape(bf16[1280,2,540]{2,1,0:T(2,128)(2,1)} %copy.33) | data formatting | bytes 5529600 | tf_op jit(solution)/shard_map/while/body/eval_jaxpr/convert_element_type | solution.py:75
  241.2 1.5 convolution_bitcast_fusion.2
  244.8 12.4 %fusion.47 = (bf16[1280,1,540]{0,2,1:T(8,128)(2,1)S(1)}, bf16[1280,1,540]{0,2,1:T(8,128)(2,1)S(1)}) fusion(s32[1280]{0:T(1024)S(1)} %get-tuple-element.302, f32[1280]{0:T(1024)S(1)} %get-tuple-element.273, f32[1280]{0:T(1024)S(1)} %get-tuple-element.274, f32[1280]{0:T(1024)S(1)} %reduce.4, f32[1280]{0:T(1024)S(1)} %reduce.5), kind=kLoop, calls=%fused_computation.12.clone.1 | loop fusion | flops 13132800 | bytes 2790400 | tf_op jit(solution)/shard_map/convert
  257.5 7.2 %copy.33 = bf16[1280,2,540]{2,1,0:T(2,128)(2,1)} copy(bf16[1280,2,540]{0,2,1:T(8,128)(2,1)S(1)} %pad_maximum_fusion.2) | data formatting | bytes 5529600 | tf_op jit(solution)/shard_map/while/body/eval_jaxpr/stack | solution.py:74
  264.7 6.6 %convert_element_type.80 = bf16[2560,540]{1,0:T(8,128)(2,1)S(1)} reshape(bf16[1280,2,540]{2,1,0:T(2,128)(2,1)} %copy.33) | data formatting | bytes 5529600 | tf_op jit(solution)/shard_map/while/body/eval_jaxpr/convert_element_type | solution.py:75
  271.3 1.5 convolution_bitcast_fusion.2
  274.9 12.4 %fusion.47 = (bf16[1280,1,540]{0,2,1:T(8,128)(2,1)S(1)}, bf16[1280,1,540]{0,2,1:T(8,128)(2,1)S(1)}) fusion(s32[1280]{0:T(1024)S(1)} %get-tuple-element.302, f32[1280]{0:T(1024)S(1)} %get-tuple-element.273, f32[1280]{0:T(1024)S(1)} %get-tuple-element.274, f32[1280]{0:T(1024)S(1)} %reduce.4, f32[1280]{0:T(1024)S(1)} %reduce.5), kind=kLoop, calls=%fused_computation.12.clone.1 | loop fusion | flops 13132800 | bytes 2790400 | tf_op jit(solution)/shard_map/convert
  287.5 7.2 %copy.33 = bf16[1280,2,540]{2,1,0:T(2,128)(2,1)} copy(bf16[1280,2,540]{0,2,1:T(8,128)(2,1)S(1)} %pad_maximum_fusion.2) | data formatting | bytes 5529600 | tf_op jit(solution)/shard_map/while/body/eval_jaxpr/stack | solution.py:74
  294.7 6.6 %convert_element_type.80 = bf16[2560,540]{1,0:T(8,128)(2,1)S(1)} reshape(bf16[1280,2,540]{2,1,0:T(2,128)(2,1)} %copy.33) | data formatting | bytes 5529600 | tf_op jit(solution)/shard_map/while/body/eval_jaxpr/convert_element_type | solution.py:75
  301.3 1.5 convolution_bitcast_fusion.2
  304.9 12.4 %fusion.47 = (bf16[1280,1,540]{0,2,1:T(8,128)(2,1)S(1)}, bf16[1280,1,540]{0,2,1:T(8,128)(2,1)S(1)}) fusion(s32[1280]{0:T(1024)S(1)} %get-tuple-element.302, f32[1280]{0:T(1024)S(1)} %get-tuple-element.273, f32[1280]{0:T(1024)S(1)} %get-tuple-element.274, f32[1280]{0:T(1024)S(1)} %reduce.4, f32[1280]{0:T(1024)S(1)} %reduce.5), kind=kLoop, calls=%fused_computation.12.clone.1 | loop fusion | flops 13132800 | bytes 2790400 | tf_op jit(solution)/shard_map/convert
  317.6 7.2 %copy.33 = bf16[1280,2,540]{2,1,0:T(2,128)(2,1)} copy(bf16[1280,2,540]{0,2,1:T(8,128)(2,1)S(1)} %pad_maximum_fusion.2) | data formatting | bytes 5529600 | tf_op jit(solution)/shard_map/while/body/eval_jaxpr/stack | solution.py:74
  324.8 6.6 %convert_element_type.80 = bf16[2560,540]{1,0:T(8,128)(2,1)S(1)} reshape(bf16[1280,2,540]{2,1,0:T(2,128)(2,1)} %copy.33) | data formatting | bytes 5529600 | tf_op jit(solution)/shard_map/while/body/eval_jaxpr/convert_element_type | solution.py:75
  331.4 1.5 convolution_bitcast_fusion.2
  335.0 12.4 %fusion.47 = (bf16[1280,1,540]{0,2,1:T(8,128)(2,1)S(1)}, bf16[1280,1,540]{0,2,1:T(8,128)(2,1)S(1)}) fusion(s32[1280]{0:T(1024)S(1)} %get-tuple-element.302, f32[1280]{0:T(1024)S(1)} %get-tuple-element.273, f32[1280]{0:T(1024)S(1)} %get-tuple-element.274, f32[1280]{0:T(1024)S(1)} %reduce.4, f32[1280]{0:T(1024)S(1)} %reduce.5), kind=kLoop, calls=%fused_computation.12.clone.1 | loop fusion | flops 13132800 | bytes 2790400 | tf_op jit(solution)/shard_map/convert
  347.7 7.2 %copy.33 = bf16[1280,2,540]{2,1,0:T(2,128)(2,1)} copy(bf16[1280,2,540]{0,2,1:T(8,128)(2,1)S(1)} %pad_maximum_fusion.2) | data formatting | bytes 5529600 | tf_op jit(solution)/shard_map/while/body/eval_jaxpr/stack | solution.py:74
  354.9 6.6 %convert_element_type.80 = bf16[2560,540]{1,0:T(8,128)(2,1)S(1)} reshape(bf16[1280,2,540]{2,1,0:T(2,128)(2,1)} %copy.33) | data formatting | bytes 5529600 | tf_op jit(solution)/shard_map/while/body/eval_jaxpr/convert_element_type | solution.py:75
  361.5 1.5 convolution_bitcast_fusion.2
  363.8 0.9 copy.22
  364.8 0.8 reshape.277
  365.6 35.4 %all-reduce.2.cloned.1.call-done = f32[2,4,4320]{2,1,0:T(4,128)} async-done(((f32[2,4,4320]{2,1,0:T(4,128)}), f32[2,4,4320]{2,1,0:T(4,128)}) %all-reduce.2.cloned.1.call-update) | async-done | bytes 138256 | tf_op jit(solution)/shard_map/psum | solution.py:90
  401.2 25.6 %all-gather.2.cloned.1.call-done = f32[16,4,4320]{2,1,0:T(4,128)} async-done(((f32[2,4,4320]{2,1,0:T(4,128)}), f32[16,4,4320]{2,1,0:T(4,128)}) %all-gather.2.cloned.1.call-update) | async-done | bytes 1105936 | tf_op jit(solution)/shard_map/all_gather | solution.py:91
  426.9 1.3 copy.23
  429.6 0.7 fusion.34
  (99 shorter events, 21.0 us)
Async XLA Ops:
  60.8 52.4 %copy-start = (s32[1280]{0:T(1024)S(1)}, s32[1280]{0:T(1024)}, u32[]{:S(2)}) copy-start(s32[1280]{0:T(1024)} %param.12) | copy-start | bytes 15364
  109.0 10.6 %all-to-all-start = ((bf16[320,8,48]{0,2,1:T(8,128)(2,1)}), bf16[320,8,48]{0,2,1:T(8,128)(2,1)S(1)}, u32[]{:S(2)}, u32[]{:S(2)}) async-start(bf16[320,8,48]{0,2,1:T(8,128)(2,1)} %copy.18), calls=%async_computation | async-start | bytes 589824 | tf_op jit(solution)/shard_map/all_to_all | solution.py:52
  113.2 287.8 %all-reduce.2.cloned.1.call-start = ((), (), s32[]{:S(2)}) async-start(), calls=%async_computation.1 | async-start | bytes 278528 | tf_op jit(solution)/shard_map/psum | solution.py:90
  113.2 10.0 %copy-start.1 = (f32[6]{0:T(128)S(1)}, f32[6]{0:T(128)}, u32[]{:S(2)}) copy-start(f32[6]{0:T(128)} %param.13) | copy-start | bytes 76
  123.3 277.8 %copy-start.2 = (f32[16]{0:T(128)S(1)}, f32[16]{0:T(128)}, u32[]{:S(2)}) copy-start(f32[16]{0:T(128)} %param.15) | copy-start | bytes 196
  123.3 277.9 %copy-start.3 = (s32[16]{0:T(128)S(1)}, s32[16]{0:T(128)}, u32[]{:S(2)}) copy-start(s32[16]{0:T(128)} %param.14) | copy-start | bytes 196
  365.6 61.3 %all-gather.2.cloned.1.call-start = ((), (), s32[]{:S(2)}) async-start(), calls=%async_computation.2 | async-start | bytes 1253376 | tf_op jit(solution)/shard_map/all_gather | solution.py:91
Sparse Core Ops, SparseCore 0:
  365.7 35.2 all-reduce.1
  403.0 23.7 all-gather.1
where the time goes:
time: 439 us; the launch traced here: 437 us
  local copies, waits for them, and re-layouts  156 us (36%)
  other arithmetic  136 us (31%)
  waiting for transfers between devices  67.4 us (15%)
  matrix products  59.3 us (14%)
  between operations  13.5 us (3%)
    another operation x24, other arithmetic  99.7 us
    another operation x8, local copies, waits for them, and re-layouts, one_block(): jnp.stack([factor * cos_vals, -factor * sin_vals], axis=1)  57.6 us
    convert_element_type x8, local copies, waits for them, and re-layouts, one_block(): fourier = jnp.stack([factor * cos_vals, -factor * sin_vals], axis=1).asty...  52.9 us
    dot_general x1, matrix products, local(): jnp.einsum('skj,slj->slk', coefficient, legendre, preferred_element_type=...  47 us
    psum x1, waiting for transfers between devices, local(): summed = lax.psum(partial_value, 'lev')  35.4 us
    unnamed x10, local copies, waits for them, and re-layouts  27.6 us
    select_n x1, other arithmetic, local(): jnp.where(in_triangle, coefficient, jnp.zeros_like(coefficient))  26.6 us
    all_gather x1, waiting for transfers between devices, local(): gathered = lax.all_gather(summed, ('wave', 'cpl'), axis=0, tiled=True)  25.6 us
  transfers between devices with their start and end apart: 3, of which 3 were waited for; matrix products, arithmetic and copies ran while one was open for 0% of the time, Pallas kernels for 0%

commit v1 on v0

--- a/solution.py
+++ b/solution.py
@@ -88,7 +88,26 @@
     weight_hi = lax.dynamic_slice_in_dim(row_weight, own_first, lat_dev)
     strip_width = NLON // lax.axis_size("lev")
     summed = lax.psum(partial_value, "lev")
-    gathered = lax.all_gather(summed, ("wave", "cpl"), axis=0, tiled=True)
+    mid_arr, res, f_next = (
+        lax.psum(1, ("wave", "cpl")),
+        lax.axis_index(("wave", "cpl")),
+        summed.shape[0],
+    )
+    y1, y2 = (summed, 1)
+    while y2 < mid_arr:
+        y1 = jnp.concatenate(
+            [
+                y1,
+                lax.ppermute(
+                    y1,
+                    ("wave", "cpl"),
+                    perm=tuple(((num, (num - y2) % mid_arr) for num in range(mid_arr))),
+                ),
+            ],
+            axis=0,
+        )
+        y2 = 2 * y2
+    gathered = jnp.roll(y1, shift=res * f_next, axis=0)
     gathered = latitude_order(gathered, wave_count, cpl_count, lat_dev)
     gathered = lax.dynamic_slice_in_dim(
         gathered, lax.axis_index("lev") * strip_width, strip_width, 2

time: 439 us -> 441 us (level)
    all_gather x1 -> x0, waiting for transfers between devices: 25.6 us -> none  [local(): gathered = lax.all_gather(summed, ('wave', 'cpl'), axis=0, tiled=True)]
    ppermute x0 -> x3, waiting for transfers between devices: none -> 22.3 us  [local(): lax.ppermute(y1, ('wave', 'cpl'), perm=tuple(((num, (num - y2) % mid_arr)...]
    unnamed x10 -> x19, local copies, waits for them, and re-layouts: 27.6 us -> 28.8 us
  transfers between devices with their start and end apart: 3 -> 5, of which waited for: 3 -> 5; matrix products, arithmetic and copies ran while one was open for 0% -> 0% of each run, Pallas kernels for 0% -> 0%
where the time goes in v1:
time: 441 us; the launch traced here: 439 us
  local copies, waits for them, and re-layouts  157 us (36%)
  other arithmetic  139 us (32%)
  waiting for transfers between devices  63.9 us (14%)
  matrix products  59.3 us (13%)
  between operations  13.6 us (3%)
  starting transfers between devices  5.84 us (1%)
    another operation x24, other arithmetic  99.7 us
    another operation x8, local copies, waits for them, and re-layouts, one_block(): jnp.stack([factor * cos_vals, -factor * sin_vals], axis=1)  58 us
    convert_element_type x8, local copies, waits for them, and re-layouts, one_block(): fourier = jnp.stack([factor * cos_vals, -factor * sin_vals], axis=1).asty...  52.9 us
    dot_general x1, matrix products, local(): jnp.einsum('skj,slj->slk', coefficient, legendre, preferred_element_type=...  47 us
    psum x1, waiting for transfers between devices, local(): summed = lax.psum(partial_value, 'lev')  35.3 us
    unnamed x19, local copies, waits for them, and re-layouts  28.8 us
    select_n x1, other arithmetic, local(): jnp.where(in_triangle, coefficient, jnp.zeros_like(coefficient))  26.6 us
    ppermute x3, waiting for transfers between devices, local(): lax.ppermute(y1, ('wave', 'cpl'), perm=tuple(((num, (num - y2) % mid_arr)...  22.3 us
  transfers between devices with their start and end apart: 5, of which 5 were waited for; matrix products, arithmetic and copies ran while one was open for 0% of the time, Pallas kernels for 0%

profile of v1, /device:TPU:0, one launch (start us, length us, event | category | flops | bytes accessed | tf_op | source)
XLA Modules:
  0.0 439.5 jit_solution(14991474685655498898)
XLA Ops:
  7.6 26.6 %copy.23 = bf16[320,2,4,6,1280]{4,0,3,2,1:T(8,128)(2,1)} copy(bf16[320,2,4,6,1280]{4,2,3,1,0:T(4,128)(2,1)} %param.10) | data formatting | bytes 78643200 | tf_op args[0]
  34.3 26.6 %bitcast_select_fusion = bf16[320,48,1280]{2,0,1:T(8,128)(2,1)} fusion(bf16[320,2,4,6,1280]{4,0,3,2,1:T(8,128)(2,1)} %copy.23, pred[320,1280]{1,0:T(8,128)(4,1)S(1)} %iota_compare_fusion), kind=kLoop, calls=%fused_computation.40 | loop fusion | flops 19660800 | bytes 79052800 | tf_op jit(solution)/shard_map/jit(_where)/select_n | solution.py:48
  60.9 47.0 %fusion.31 = bf16[320,8,48]{2,1,0:T(8,128)(2,1)S(1)} fusion(bf16[320,8,1280]{2,1,0:T(8,128)(2,1)} %param.11, bf16[320,48,1280]{2,0,1:T(8,128)(2,1)} %bitcast_select_fusion), kind=kOutput, calls=%fused_computation.45 | convolution fusion | flops 314695680 | bytes 46120960 | tf_op jit(solution)/shard_map/skj,slj->slk/dot_general | solution.py:49
  107.9 1.1 copy.25
  109.0 4.2 all-to-all-start
  113.4 6.2 %all-to-all-done = bf16[320,8,48]{0,2,1:T(8,128)(2,1)S(1)} async-done(((bf16[320,8,48]{0,2,1:T(8,128)(2,1)}), bf16[320,8,48]{0,2,1:T(8,128)(2,1)S(1)}, u32[]{:S(2)}, u32[]{:S(2)}) %all-to-all-start) | async-done | bytes 245792 | tf_op jit(solution)/shard_map/all_to_all | solution.py:52
  120.1 1.7 copy.27
  123.3 242.5 %while.14 = (s32[]{:T(128)}, f32[8,2,4,540]{3,2,1,0:T(4,128)}, f32[6]{0:T(128)S(1)}, f32[1280,1]{0,1:T(1,128)S(1)}, s32[8]{0:T(128)S(1)}, /*index=5*/s32[1280]{0...) while((s32[]{:T(128)}, f32[8,2,4,540]{3,2,1,0:T(4,128)}, ...), condition=%wide.region_2.3_spmd.clone.clone, body=%wide.region_0.2_spmd.clone.clone.sunk | while | flops 147317040 | bytes 22999700 | solution.py:84
  124.8 12.4 %fusion.47 = (bf16[1280,1,540]{0,2,1:T(8,128)(2,1)S(1)}, bf16[1280,1,540]{0,2,1:T(8,128)(2,1)S(1)}) fusion(s32[1280]{0:T(1024)S(1)} %get-tuple-element.310, f32[1280]{0:T(1024)S(1)} %get-tuple-element.281, f32[1280]{0:T(1024)S(1)} %get-tuple-element.282, f32[1280]{0:T(1024)S(1)} %reduce.4, f32[1280]{0:T(1024)S(1)} %reduce.5), kind=kLoop, calls=%fused_computation.12.clone.1 | loop fusion | flops 13132800 | bytes 2790400 | tf_op jit(solution)/shard_map/convert
  137.5 7.2 %copy.40 = bf16[1280,2,540]{2,1,0:T(2,128)(2,1)} copy(bf16[1280,2,540]{0,2,1:T(8,128)(2,1)S(1)} %pad_maximum_fusion.4) | data formatting | bytes 5529600 | tf_op jit(solution)/shard_map/while/body/eval_jaxpr/stack | solution.py:74
  144.7 6.6 %convert_element_type.80 = bf16[2560,540]{1,0:T(8,128)(2,1)S(1)} reshape(bf16[1280,2,540]{2,1,0:T(2,128)(2,1)} %copy.40) | data formatting | bytes 5529600 | tf_op jit(solution)/shard_map/while/body/eval_jaxpr/convert_element_type | solution.py:75
  151.3 1.5 convolution_bitcast_fusion.2
  155.1 12.4 %fusion.47 = (bf16[1280,1,540]{0,2,1:T(8,128)(2,1)S(1)}, bf16[1280,1,540]{0,2,1:T(8,128)(2,1)S(1)}) fusion(s32[1280]{0:T(1024)S(1)} %get-tuple-element.310, f32[1280]{0:T(1024)S(1)} %get-tuple-element.281, f32[1280]{0:T(1024)S(1)} %get-tuple-element.282, f32[1280]{0:T(1024)S(1)} %reduce.4, f32[1280]{0:T(1024)S(1)} %reduce.5), kind=kLoop, calls=%fused_computation.12.clone.1 | loop fusion | flops 13132800 | bytes 2790400 | tf_op jit(solution)/shard_map/convert
  167.8 7.2 %copy.40 = bf16[1280,2,540]{2,1,0:T(2,128)(2,1)} copy(bf16[1280,2,540]{0,2,1:T(8,128)(2,1)S(1)} %pad_maximum_fusion.4) | data formatting | bytes 5529600 | tf_op jit(solution)/shard_map/while/body/eval_jaxpr/stack | solution.py:74
  175.0 6.6 %convert_element_type.80 = bf16[2560,540]{1,0:T(8,128)(2,1)S(1)} reshape(bf16[1280,2,540]{2,1,0:T(2,128)(2,1)} %copy.40) | data formatting | bytes 5529600 | tf_op jit(solution)/shard_map/while/body/eval_jaxpr/convert_element_type | solution.py:75
  181.6 1.5 convolution_bitcast_fusion.2
  185.4 12.4 %fusion.47 = (bf16[1280,1,540]{0,2,1:T(8,128)(2,1)S(1)}, bf16[1280,1,540]{0,2,1:T(8,128)(2,1)S(1)}) fusion(s32[1280]{0:T(1024)S(1)} %get-tuple-element.310, f32[1280]{0:T(1024)S(1)} %get-tuple-element.281, f32[1280]{0:T(1024)S(1)} %get-tuple-element.282, f32[1280]{0:T(1024)S(1)} %reduce.4, f32[1280]{0:T(1024)S(1)} %reduce.5), kind=kLoop, calls=%fused_computation.12.clone.1 | loop fusion | flops 13132800 | bytes 2790400 | tf_op jit(solution)/shard_map/convert
  198.1 7.2 %copy.40 = bf16[1280,2,540]{2,1,0:T(2,128)(2,1)} copy(bf16[1280,2,540]{0,2,1:T(8,128)(2,1)S(1)} %pad_maximum_fusion.4) | data formatting | bytes 5529600 | tf_op jit(solution)/shard_map/while/body/eval_jaxpr/stack | solution.py:74
  205.3 6.6 %convert_element_type.80 = bf16[2560,540]{1,0:T(8,128)(2,1)S(1)} reshape(bf16[1280,2,540]{2,1,0:T(2,128)(2,1)} %copy.40) | data formatting | bytes 5529600 | tf_op jit(solution)/shard_map/while/body/eval_jaxpr/convert_element_type | solution.py:75
  212.0 1.5 convolution_bitcast_fusion.2
  215.7 12.4 %fusion.47 = (bf16[1280,1,540]{0,2,1:T(8,128)(2,1)S(1)}, bf16[1280,1,540]{0,2,1:T(8,128)(2,1)S(1)}) fusion(s32[1280]{0:T(1024)S(1)} %get-tuple-element.310, f32[1280]{0:T(1024)S(1)} %get-tuple-element.281, f32[1280]{0:T(1024)S(1)} %get-tuple-element.282, f32[1280]{0:T(1024)S(1)} %reduce.4, f32[1280]{0:T(1024)S(1)} %reduce.5), kind=kLoop, calls=%fused_computation.12.clone.1 | loop fusion | flops 13132800 | bytes 2790400 | tf_op jit(solution)/shard_map/convert
  228.4 7.2 %copy.40 = bf16[1280,2,540]{2,1,0:T(2,128)(2,1)} copy(bf16[1280,2,540]{0,2,1:T(8,128)(2,1)S(1)} %pad_maximum_fusion.4) | data formatting | bytes 5529600 | tf_op jit(solution)/shard_map/while/body/eval_jaxpr/stack | solution.py:74
  235.6 6.6 %convert_element_type.80 = bf16[2560,540]{1,0:T(8,128)(2,1)S(1)} reshape(bf16[1280,2,540]{2,1,0:T(2,128)(2,1)} %copy.40) | data formatting | bytes 5529600 | tf_op jit(solution)/shard_map/while/body/eval_jaxpr/convert_element_type | solution.py:75
  242.3 1.5 convolution_bitcast_fusion.2
  246.0 12.4 %fusion.47 = (bf16[1280,1,540]{0,2,1:T(8,128)(2,1)S(1)}, bf16[1280,1,540]{0,2,1:T(8,128)(2,1)S(1)}) fusion(s32[1280]{0:T(1024)S(1)} %get-tuple-element.310, f32[1280]{0:T(1024)S(1)} %get-tuple-element.281, f32[1280]{0:T(1024)S(1)} %get-tuple-element.282, f32[1280]{0:T(1024)S(1)} %reduce.4, f32[1280]{0:T(1024)S(1)} %reduce.5), kind=kLoop, calls=%fused_computation.12.clone.1 | loop fusion | flops 13132800 | bytes 2790400 | tf_op jit(solution)/shard_map/convert
  258.7 7.2 %copy.40 = bf16[1280,2,540]{2,1,0:T(2,128)(2,1)} copy(bf16[1280,2,540]{0,2,1:T(8,128)(2,1)S(1)} %pad_maximum_fusion.4) | data formatting | bytes 5529600 | tf_op jit(solution)/shard_map/while/body/eval_jaxpr/stack | solution.py:74
  266.0 6.6 %convert_element_type.80 = bf16[2560,540]{1,0:T(8,128)(2,1)S(1)} reshape(bf16[1280,2,540]{2,1,0:T(2,128)(2,1)} %copy.40) | data formatting | bytes 5529600 | tf_op jit(solution)/shard_map/while/body/eval_jaxpr/convert_element_type | solution.py:75
  272.6 1.5 convolution_bitcast_fusion.2
  276.4 12.4 %fusion.47 = (bf16[1280,1,540]{0,2,1:T(8,128)(2,1)S(1)}, bf16[1280,1,540]{0,2,1:T(8,128)(2,1)S(1)}) fusion(s32[1280]{0:T(1024)S(1)} %get-tuple-element.310, f32[1280]{0:T(1024)S(1)} %get-tuple-element.281, f32[1280]{0:T(1024)S(1)} %get-tuple-element.282, f32[1280]{0:T(1024)S(1)} %reduce.4, f32[1280]{0:T(1024)S(1)} %reduce.5), kind=kLoop, calls=%fused_computation.12.clone.1 | loop fusion | flops 13132800 | bytes 2790400 | tf_op jit(solution)/shard_map/convert
  289.0 7.2 %copy.40 = bf16[1280,2,540]{2,1,0:T(2,128)(2,1)} copy(bf16[1280,2,540]{0,2,1:T(8,128)(2,1)S(1)} %pad_maximum_fusion.4) | data formatting | bytes 5529600 | tf_op jit(solution)/shard_map/while/body/eval_jaxpr/stack | solution.py:74
  296.3 6.6 %convert_element_type.80 = bf16[2560,540]{1,0:T(8,128)(2,1)S(1)} reshape(bf16[1280,2,540]{2,1,0:T(2,128)(2,1)} %copy.40) | data formatting | bytes 5529600 | tf_op jit(solution)/shard_map/while/body/eval_jaxpr/convert_element_type | solution.py:75
  302.9 1.5 convolution_bitcast_fusion.2
  306.7 12.4 %fusion.47 = (bf16[1280,1,540]{0,2,1:T(8,128)(2,1)S(1)}, bf16[1280,1,540]{0,2,1:T(8,128)(2,1)S(1)}) fusion(s32[1280]{0:T(1024)S(1)} %get-tuple-element.310, f32[1280]{0:T(1024)S(1)} %get-tuple-element.281, f32[1280]{0:T(1024)S(1)} %get-tuple-element.282, f32[1280]{0:T(1024)S(1)} %reduce.4, f32[1280]{0:T(1024)S(1)} %reduce.5), kind=kLoop, calls=%fused_computation.12.clone.1 | loop fusion | flops 13132800 | bytes 2790400 | tf_op jit(solution)/shard_map/convert
  319.3 7.2 %copy.40 = bf16[1280,2,540]{2,1,0:T(2,128)(2,1)} copy(bf16[1280,2,540]{0,2,1:T(8,128)(2,1)S(1)} %pad_maximum_fusion.4) | data formatting | bytes 5529600 | tf_op jit(solution)/shard_map/while/body/eval_jaxpr/stack | solution.py:74
  326.6 6.6 %convert_element_type.80 = bf16[2560,540]{1,0:T(8,128)(2,1)S(1)} reshape(bf16[1280,2,540]{2,1,0:T(2,128)(2,1)} %copy.40) | data formatting | bytes 5529600 | tf_op jit(solution)/shard_map/while/body/eval_jaxpr/convert_element_type | solution.py:75
  333.2 1.5 convolution_bitcast_fusion.2
  337.0 12.4 %fusion.47 = (bf16[1280,1,540]{0,2,1:T(8,128)(2,1)S(1)}, bf16[1280,1,540]{0,2,1:T(8,128)(2,1)S(1)}) fusion(s32[1280]{0:T(1024)S(1)} %get-tuple-element.310, f32[1280]{0:T(1024)S(1)} %get-tuple-element.281, f32[1280]{0:T(1024)S(1)} %get-tuple-element.282, f32[1280]{0:T(1024)S(1)} %reduce.4, f32[1280]{0:T(1024)S(1)} %reduce.5), kind=kLoop, calls=%fused_computation.12.clone.1 | loop fusion | flops 13132800 | bytes 2790400 | tf_op jit(solution)/shard_map/convert
  349.6 7.2 %copy.40 = bf16[1280,2,540]{2,1,0:T(2,128)(2,1)} copy(bf16[1280,2,540]{0,2,1:T(8,128)(2,1)S(1)} %pad_maximum_fusion.4) | data formatting | bytes 5529600 | tf_op jit(solution)/shard_map/while/body/eval_jaxpr/stack | solution.py:74
  356.9 6.6 %convert_element_type.80 = bf16[2560,540]{1,0:T(8,128)(2,1)S(1)} reshape(bf16[1280,2,540]{2,1,0:T(2,128)(2,1)} %copy.40) | data formatting | bytes 5529600 | tf_op jit(solution)/shard_map/while/body/eval_jaxpr/convert_element_type | solution.py:75
  363.5 1.5 convolution_bitcast_fusion.2
  367.7 35.3 %all-reduce.2.cloned.1.call-done = f32[2,4,4320]{2,1,0:T(4,128)} async-done(((f32[2,4,4320]{2,1,0:T(4,128)}), f32[2,4,4320]{2,1,0:T(4,128)}) %all-reduce.2.cloned.1.call-update) | async-done | bytes 138256 | tf_op jit(solution)/shard_map/psum | solution.py:90
  403.1 1.0 constant_dynamic-update-slice_fusion.7
  404.1 4.2 collective-permute-done
  408.3 1.0 pad_maximum_fusion.2
  409.8 4.0 collective-permute-done.1
  413.8 1.0 pad_maximum_fusion.1
  414.8 1.2 collective-permute-start.2
  416.0 14.0 %collective-permute-done.2 = f32[8,4,4320]{2,1,0:T(4,128)S(1)} collective-permute-done((f32[8,4,4320]{2,1,0:T(4,128)S(1)}, f32[8,4,4320]{2,1,0:T(4,128)S(1)}, u32[]{:S(2)}, u32[]{:S(2)}) %collective-permute-start.2) | collective-permute-done | bytes 552992 | tf_op jit(solution)/shard_map/ppermute | solution.py:101
  (115 shorter events, 27.6 us)
Async XLA Ops:
  60.9 52.4 %copy-start.1 = (s32[1280]{0:T(1024)S(1)}, s32[1280]{0:T(1024)}, u32[]{:S(2)}) copy-start(s32[1280]{0:T(1024)} %param.12) | copy-start | bytes 15364
  60.9 52.4 %copy-start.3 = (s32[16]{0:T(128)S(1)}, s32[16]{0:T(128)}, u32[]{:S(2)}) copy-start(s32[16]{0:T(128)} %param.14) | copy-start | bytes 196
  109.0 10.6 %all-to-all-start = ((bf16[320,8,48]{0,2,1:T(8,128)(2,1)}), bf16[320,8,48]{0,2,1:T(8,128)(2,1)S(1)}, u32[]{:S(2)}, u32[]{:S(2)}) async-start(bf16[320,8,48]{0,2,1:T(8,128)(2,1)} %copy.25), calls=%async_computation | async-start | bytes 589824 | tf_op jit(solution)/shard_map/all_to_all | solution.py:52
  113.3 289.8 %all-reduce.2.cloned.1.call-start = ((), (), s32[]{:S(2)}) async-start(), calls=%async_computation.1 | async-start | bytes 278528 | tf_op jit(solution)/shard_map/psum | solution.py:90
  113.3 10.0 %copy-start.2 = (f32[6]{0:T(128)S(1)}, f32[6]{0:T(128)}, u32[]{:S(2)}) copy-start(f32[6]{0:T(128)} %param.13) | copy-start | bytes 76
  123.3 244.3 %copy-start.4 = (f32[16]{0:T(128)S(1)}, f32[16]{0:T(128)}, u32[]{:S(2)}) copy-start(f32[16]{0:T(128)} %param.15) | copy-start | bytes 196
  403.1 27.1 %copy-start = (f32[2,4,4320]{2,1,0:T(4,128)S(1)}, f32[2,4,4320]{2,1,0:T(4,128)}, u32[]{:S(2)}) copy-start(f32[2,4,4320]{2,1,0:T(4,128)} %all-reduce.2.cloned.1.call-done) | copy-start | bytes 414724
  403.1 5.3 %collective-permute-start = (f32[2,4,4320]{2,1,0:T(4,128)}, f32[2,4,4320]{2,1,0:T(4,128)S(1)}, u32[]{:S(2)}, u32[]{:S(2)}) collective-permute-start(f32[2,4,4320]{2,1,0:T(4,128)} %all-reduce.2.cloned.1.call-done), channel_id=1, source_target_pairs={{0,25},{1,0},{8,1},{9,8},{16,9},{17,16},{24,17},{25,24},{2,27},{3,... | collective-permute-start | bytes 414728 | tf_op jit(solution)/shard_map/ppermute | solution.py:101
  409.3 4.5 %collective-permute-start.1 = (f32[4,4,4320]{2,1,0:T(4,128)S(1)}, f32[4,4,4320]{2,1,0:T(4,128)S(1)}, u32[]{:S(2)}, u32[]{:S(2)}) collective-permute-start(f32[4,4,4320]{2,1,0:T(4,128)S(1)} %pad_maximum_fusion.2), channel_id=1, source_target_pairs={{0,24},{1,25},{8,0},{9,1},{16,8},{17,9},{24,16},{25,17},{2,26},{3,... | collective-permute-start | bytes 829448 | tf_op jit(solution)/shard_map/ppermute | solution.py:101
  414.8 15.2 %collective-permute-start.2 = (f32[8,4,4320]{2,1,0:T(4,128)S(1)}, f32[8,4,4320]{2,1,0:T(4,128)S(1)}, u32[]{:S(2)}, u32[]{:S(2)}) collective-permute-start(f32[8,4,4320]{2,1,0:T(4,128)S(1)} %pad_maximum_fusion.1), channel_id=1, source_target_pairs={{0,16},{1,17},{8,24},{9,25},{16,0},{17,1},{24,8},{25,9},{2,18},{3,... | collective-permute-start | bytes 1658888 | tf_op jit(solution)/shard_map/ppermute | solution.py:101
Sparse Core Ops, SparseCore 0:
  367.7 35.2 all-reduce.1
